TPU v7x, 128 devices: a whole 4x4x4 slice. The times are simulated.
128 devices in a mesh: sec: 2 (over x_hi), head: 4 (over x_lo, core), ctx: 16 (over z, y).
Axes of the slice: x: 4 (x_hi: 2, x_lo: 2; x = x_hi * 2 + x_lo), y: 4, z: 4, core: 2. Of those that a mesh axis runs over, the one named last changes fastest.
Arguments:
- proposal_rows: bfloat16 [512, 8192], P('sec', 'ctx'), may hold values from -400 to 400
- norm_gain: bfloat16 [8192], P('ctx'), may hold values from 0.25 to 1.75
- query_weight: bfloat16 [8192, 8192], P('ctx', ('sec', 'head')), may hold values from -0.0625 to 0.0625
- key_weight: bfloat16 [8192, 8, 128], P('ctx', ('sec', 'head')), may hold values from -0.25 to 0.25
- value_weight: bfloat16 [8192, 8, 128], P('ctx', ('sec', 'head')), may hold values from -0.0625 to 0.0625
- out_weight: bfloat16 [8192, 8192], P(('sec', 'head'), 'ctx'), may hold values from -0.0625 to 0.0625
- context_keys: bfloat16 [32768, 8, 128], P('ctx', ('sec', 'head')), may hold values from -256 to 256
- context_values: bfloat16 [32768, 8, 128], P('ctx', ('sec', 'head')), may hold values from -5 to 5
- prefix_lengths: int32 [32], replicated, may hold values from 2048 to 32768, as said below
- parents: int32 [512], replicated, may hold values from -1 to 510, as said below
Outputs:
- block_output: bfloat16 [512, 8192], P(('sec', 'head'), 'ctx')
Inputs may be any that keep to these rules, and one draw needn't show every extreme that they name: `parents`: token i = 16 p + s of particle p has parent -1 when s = 0, else 16 q + s - 1 for some particle q <= p. `prefix_lengths`: some particle sees the whole context.
All inputs are finite; a program needn't handle non-finite values.
Results may differ from a plain program's by a relative error of at most 0.015.
The roundings to bfloat16 on the way count: a program that leaves them out, or rounds other values in their place, can miss the bound.
Values may be sent and summed in bfloat16 or wider, within the bound.
No kernel may reach another device: no remote copies, remote signals or barrier semaphores. Data moves between devices by JAX's collectives and lax.ppermute only.
A program may use at most 192 MiB of HBM per device.

v0:
```python
import math
import jax
import jax.numpy as jnp
from jax import lax
from jax.sharding import PartitionSpec as P

D = 8192
PROPOSALS = 16
NEGATIVE = -1e30
EPSILON = 1e-05


def ancestry_columns(parents, column_offset, column_amount):
    total = parents.shape[0]
    index = jnp.arange(total, dtype=jnp.int32)
    step = jnp.logical_or(parents[:, None] == index[None, :], index[:, None] == index[None, :])
    reach = step.astype(jnp.bfloat16)
    for _ in range(3):
        reach = (jnp.dot(reach, reach, preferred_element_type=jnp.float32) > 0).astype(jnp.bfloat16)
    columns = lax.dynamic_slice_in_dim(reach, column_offset, column_amount, 1)
    return jnp.dot(reach, columns, preferred_element_type=jnp.float32) > 0


def body(
    proposal_rows,
    norm_gain,
    query_weight,
    key_weight,
    value_weight,
    out_weight,
    context_keys,
    context_values,
    prefix_lengths,
    parents,
):
    gathered = lax.all_gather(proposal_rows, "sec", axis=0, tiled=True)
    gathered_wide = gathered.astype(jnp.float32)
    total_rows = gathered.shape[0]
    squares = jnp.sum(gathered_wide * gathered_wide, axis=1)
    scaled = (gathered_wide * norm_gain.astype(jnp.float32)[None, :]).astype(jnp.bfloat16)
    query_width = query_weight.shape[1]
    head_size = key_weight.shape[2]
    groups = query_width // head_size
    joined = jnp.concatenate([query_weight, key_weight[:, 0, :], value_weight[:, 0, :]], axis=1)
    partial_value = jnp.dot(scaled, joined, preferred_element_type=jnp.float32)
    proj_width = partial_value.shape[1]
    lane = jnp.arange(128, dtype=jnp.int32)
    square_block = jnp.where(lane[None, :] == 0, squares[:, None], 0.0)
    packed = jnp.concatenate([partial_value, square_block], axis=1)
    reduced = lax.psum_scatter(packed, "ctx", scatter_dimension=0, tiled=True)
    row_share = reduced.shape[0]
    inverse = lax.rsqrt(reduced[:, proj_width] / D + EPSILON)[:, None]
    settled = reduced[:, :proj_width] * inverse
    own_queries = settled[:, :query_width].astype(jnp.bfloat16)
    tree_keys = settled[:, query_width : query_width + head_size].astype(jnp.bfloat16)
    tree_vals = settled[:, query_width + head_size :].astype(jnp.bfloat16)
    queries = lax.all_gather(own_queries, "ctx", axis=0, tiled=True)
    position = lax.axis_index("ctx")
    keys = context_keys[:, 0, :]
    vals = context_values[:, 0, :]
    span = keys.shape[0]
    factor = 1.0 / math.sqrt(head_size)
    grouped = queries.reshape(total_rows, groups, head_size)
    lengths_rows = jnp.repeat(prefix_lengths, PROPOSALS)
    positions = position * span + jnp.arange(span, dtype=jnp.int32)
    visible = (positions[None, :] < lengths_rows[:, None])[:, None, :]
    scores = jnp.einsum("rgd,td->rgt", grouped, keys, preferred_element_type=jnp.float32) * factor
    tree_visible = ancestry_columns(parents, position * row_share, row_share)[:, None, :]
    tree_scores = (
        jnp.einsum("rgd,td->rgt", grouped, tree_keys, preferred_element_type=jnp.float32) * factor
    )
    local_high = jnp.maximum(
        jnp.max(jnp.where(visible, scores, NEGATIVE), axis=2),
        jnp.max(jnp.where(tree_visible, tree_scores, NEGATIVE), axis=2),
    )
    highest = lax.pmax(local_high, "ctx")
    weights = jnp.where(visible, jnp.exp(scores - highest[:, :, None]), 0.0)
    tree_weights = jnp.where(tree_visible, jnp.exp(tree_scores - highest[:, :, None]), 0.0)
    weight_sum = jnp.sum(weights, axis=2) + jnp.sum(tree_weights, axis=2)
    summed = jnp.einsum(
        "rgt,td->rgd", weights.astype(jnp.bfloat16), vals, preferred_element_type=jnp.float32
    ) + jnp.einsum(
        "rgt,td->rgd",
        tree_weights.astype(jnp.bfloat16),
        tree_vals,
        preferred_element_type=jnp.float32,
    )
    sum_block = jnp.concatenate(
        [weight_sum, jnp.zeros((total_rows, 128 - groups), jnp.float32)], axis=1
    )
    packed_attn = jnp.concatenate([summed.reshape(total_rows, query_width), sum_block], axis=1)
    merged = lax.psum_scatter(packed_attn, "ctx", scatter_dimension=0, tiled=True)
    own_attended = (
        (
            merged[:, :query_width].reshape(row_share, groups, head_size)
            / merged[:, query_width : query_width + groups][:, :, None]
        )
        .reshape(row_share, query_width)
        .astype(jnp.bfloat16)
    )
    attended = lax.all_gather(own_attended, "ctx", axis=0, tiled=True)
    return lax.psum_scatter(
        jnp.dot(attended, out_weight, preferred_element_type=jnp.float32).astype(jnp.bfloat16),
        ("sec", "head"),
        scatter_dimension=0,
        tiled=True,
    )


def solution(mesh):
    placed = (
        P("sec", "ctx"),
        P("ctx"),
        P("ctx", ("sec", "head")),
        P("ctx", ("sec", "head"), None),
        P("ctx", ("sec", "head"), None),
        P(("sec", "head"), "ctx"),
        P("ctx", ("sec", "head"), None),
        P("ctx", ("sec", "head"), None),
        P(),
        P(),
    )
    return jax.shard_map(
        body, mesh=mesh, in_specs=placed, out_specs=P(("sec", "head"), "ctx"), check_vma=False
    )
```

profile of v0, /device:TPU:0, one launch (start us, length us, event | category | flops | bytes accessed | tf_op | source)
XLA Modules:
  0.0 426.5 jit_solution(10706751456148544928)
XLA Ops:
  6.5 0.0 copy-start
  6.5 0.0 reduce-scatter.6.cloned.1.call-start
  6.5 10.5 %all_gather.9 = bf16[512,512]{1,0:T(8,128)(2,1)S(1)} all-gather(bf16[256,512]{1,0:T(8,128)(2,1)} %param.10), channel_id=1, replica_groups=mesh['sec'=2,'head'=4,'ctx'=16] {'sec'}, dimensions={0}, use_global_device_ids=true | all-gather | bytes 786432 | tf_op jit(solution)/shard_map/all_gather | solution.py:36
  17.0 0.7 convert_element_type.29
  17.7 0.2 fusion.12
  17.9 0.1 broadcast_select_fusion
  18.0 2.2 fusion.5
  20.3 1.8 pad_maximum_fusion
  22.1 0.0 copy-start.2
  22.1 0.0 copy-start.3
  22.1 0.0 reduce-scatter.6.cloned.1.call-update
  22.1 0.0 all-gather.3.cloned.1.call-start
  22.1 79.1 %reduce-scatter.6.cloned.1.call-done = f32[32,1408]{1,0:T(8,128)} async-done(((f32[512,1408]{1,0:T(8,128)}), f32[32,1408]{1,0:T(8,128)}) %reduce-scatter.6.cloned.1.call-update) | async-done | bytes 180240 | tf_op jit(solution)/shard_map/reduce_scatter | solution.py:50
  101.3 0.8 fusion.37
  102.1 1.0 fusion.34
  103.1 0.6 slice.33
  103.7 0.0 all-gather.3.cloned.1.call-update
  103.8 0.0 reduce-scatter.10.cloned.1.call-start
  103.8 0.0 copy-done.2
  103.8 0.1 broadcast_in_dim.76
  103.9 0.1 lt.23
  104.0 0.1 pad.2.clone
  104.1 0.0 copy-done.3
  104.1 0.6 convolution_compare_fusion.2
  104.7 0.0 copy-start.1
  104.7 1.1 convolution_compare_fusion
  105.9 0.4 convolution_compare_fusion.3
  106.3 0.7 broadcast_compare_fusion
  106.9 38.8 %all-gather.3.cloned.1.call-done = bf16[512,1024]{1,0:T(8,128)(2,1)} async-done(((bf16[32,1024]{1,0:T(8,128)(2,1)}), bf16[512,1024]{1,0:T(8,128)(2,1)}) %all-gather.3.cloned.1.call-update) | async-done | bytes 1048592 | tf_op jit(solution)/shard_map/all_gather | solution.py:57
  145.7 1.7 select_reduce_fusion.1
  147.4 0.0 copy-done.1
  147.4 15.1 %select_reduce_fusion = (f32[512,8]{0,1:T(8,128)S(1)}, f32[512,8,2048]{2,0,1:T(8,128)}) fusion(pred[512,2048]{1,0:T(8,128)(4,1)S(1)} %broadcast_compare_fusion, bf16[2048,1,128]{2,0,1:T(8,128)(2,1)S(1)} %copy-done.1, bf16[512,1024]{1,0:T(8,128)(2,1)} %all-gather.3.cloned.1.call-done), kind=kOutput, calls=%fused_computation.1 | convolution fusion | flops 2172645376 | bytes 36192256 | tf_op jit(solution)/shard_map/rgd,td->rgt/dot_general | solution.py:67
  162.5 72.1 %pmax.7 = f32[512,8]{0,1:T(8,128)S(1)} all-reduce(f32[512,8]{0,1:T(8,128)S(1)} %max.5), channel_id=1, replica_groups=mesh['sec'=2,'head'=4,'ctx'=16] {'ctx'}, use_global_device_ids=true, to_apply=%region_4.5 | all-reduce | flops 4096 | bytes 32768 | tf_op jit(solution)/shard_map/pmax | solution.py:76
  234.6 15.2 %fusion = f32[512,8]{0,1:T(8,128)S(1)} fusion(f32[512,8,2048]{2,0,1:T(8,128)} %get-tuple-element.6, f32[512,8]{0,1:T(8,128)S(1)} %pmax.7, pred[512,2048]{1,0:T(8,128)(4,1)S(1)} %broadcast_compare_fusion), kind=kLoop, calls=%fused_computation.2 | loop fusion | flops 33550336 | bytes 34635776 | tf_op jit(solution)/shard_map/reduce_sum | solution.py:79
  249.8 15.4 %fusion.2 = f32[512,8,128]{0,2,1:T(8,128)} fusion(f32[512,8,2048]{2,0,1:T(8,128)} %get-tuple-element.6, f32[512,8]{0,1:T(8,128)S(1)} %pmax.7, pred[512,2048]{1,0:T(8,128)(4,1)S(1)} %broadcast_compare_fusion, bf16[2048,1,128]{2,0,1:T(8,128)(2,1)} %param.17), kind=kOutput, calls=%fused_computation.4 | convolution fusion | flops 2181038080 | bytes 37240832 | tf_op jit(solution)/shard_map/rgt,td->rgd/dot_general | solution.py:80
  265.2 0.1 fusion.27
  265.3 2.1 convolution_add_fusion
  267.4 0.2 maximum_maximum_fusion
  267.7 2.0 copy.25
  269.6 0.0 reduce-scatter.10.cloned.1.call-update
  269.7 0.0 all-gather.5.cloned.1.call-start
  269.7 72.2 %reduce-scatter.10.cloned.1.call-done = f32[32,1152]{1,0:T(8,128)} async-done(((f32[512,1152]{1,0:T(8,128)}), f32[32,1152]{1,0:T(8,128)}) %reduce-scatter.10.cloned.1.call-update) | async-done | bytes 147472
  341.9 0.9 slice.36
  342.8 0.2 copy.27
  343.0 0.7 slice.37
  343.7 0.1 copy.28
  343.8 0.1 fusion.22
  343.8 0.8 copy.21
  344.6 0.0 all-gather.5.cloned.1.call-update
  344.6 0.0 reduce-scatter.8.cloned.1.call-start
  344.7 42.0 %all-gather.5.cloned.1.call-done = bf16[512,1024]{1,0:T(8,128)(2,1)} async-done(((bf16[32,1024]{1,0:T(8,128)(2,1)}), bf16[512,1024]{1,0:T(8,128)(2,1)}) %all-gather.5.cloned.1.call-update) | async-done | bytes 1048592 | tf_op jit(solution)/shard_map/all_gather | solution.py:101
  386.6 0.0 copy-done
  386.6 2.8 convolution_convert_fusion
  389.4 0.0 reduce-scatter.8.cloned.1.call-update
  389.4 30.6 %reduce-scatter.8.cloned.1.call-done = bf16[64,512]{1,0:T(8,128)(2,1)} async-done(((bf16[512,512]{1,0:T(8,128)(2,1)}), bf16[64,512]{1,0:T(8,128)(2,1)}) %reduce-scatter.8.cloned.1.call-update) | async-done | bytes 65552 | tf_op jit(solution)/shard_map/reduce_scatter | solution.py:102
  (5 shorter events, 0.0 us)
Async XLA Ops:
  6.5 380.1 %copy-start = (bf16[1024,512]{1,0:T(8,128)(2,1)S(1)}, bf16[1024,512]{1,0:T(8,128)(2,1)}, u32[]{:S(2)}) copy-start(bf16[1024,512]{1,0:T(8,128)(2,1)} %param.15) | copy-start | bytes 3145732
  6.5 94.7 %reduce-scatter.6.cloned.1.call-start = ((), (), s32[]{:S(2)}) async-start(), calls=%async_computation.3 | async-start | bytes 3063808 | tf_op jit(solution)/shard_map/reduce_scatter | solution.py:50
  22.1 81.8 %copy-start.2 = (s32[32]{0:T(128)S(1)}, s32[32]{0:T(128)}, u32[]{:S(2)}) copy-start(s32[32]{0:T(128)} %param.18) | copy-start | bytes 388
  22.1 82.0 %copy-start.3 = (s32[512]{0:T(512)S(1)}, s32[512]{0:T(512)}, u32[]{:S(2)}) copy-start(s32[512]{0:T(512)} %param.19) | copy-start | bytes 6148
  22.1 123.6 %all-gather.3.cloned.1.call-start = ((), (), s32[]{:S(2)}) async-start(), calls=%async_computation.4 | async-start | bytes 1114112 | tf_op jit(solution)/shard_map/all_gather | solution.py:57
  103.8 238.1 %reduce-scatter.10.cloned.1.call-start = ((), (), s32[]{:S(2)}) async-start(), calls=%async_computation.7 | async-start | bytes 2506752
  104.7 42.7 %copy-start.1 = (bf16[2048,1,128]{2,0,1:T(8,128)(2,1)S(1)}, bf16[2048,1,128]{2,0,1:T(8,128)(2,1)}, u32[]{:S(2)}) copy-start(bf16[2048,1,128]{2,0,1:T(8,128)(2,1)} %param.16) | copy-start | bytes 1572868
  269.7 117.0 %all-gather.5.cloned.1.call-start = ((), (), s32[]{:S(2)}) async-start(), calls=%async_computation.5 | async-start | bytes 1114112 | tf_op jit(solution)/shard_map/all_gather | solution.py:101
  344.6 75.4 %reduce-scatter.8.cloned.1.call-start = ((), (), s32[]{:S(2)}) async-start(), calls=%async_computation.6 | async-start | bytes 589824 | tf_op jit(solution)/shard_map/reduce_scatter | solution.py:102
Sparse Core Ops, SparseCore 0:
  22.2 79.0 reduce-scatter.5
  103.9 41.7 all-gather.2
  269.8 72.0 reduce-scatter.9
  344.7 41.8 all-gather.4
  389.5 30.4 reduce-scatter.7
where the time goes:
time: 427 us
  waiting for transfers between devices  263 us (62%)
  blocking collectives  82.6 us (19%)
  matrix products  41.4 us (10%)
  other arithmetic  20.8 us (5%)
  between operations  13.3 us (3%)
  local copies, waits for them, and re-layouts  5.52 us (1%)
    reduce_scatter x1, waiting for transfers between devices, body(): reduced = lax.psum_scatter(packed, 'ctx', scatter_dimension=0, tiled=True)  79.1 us
    unnamed x6, waiting for transfers between devices  72.2 us
    pmax x1, blocking collectives, body(): highest = lax.pmax(local_high, 'ctx')  72.1 us
    all_gather x1, waiting for transfers between devices, body(): attended = lax.all_gather(own_attended, 'ctx', axis=0, tiled=True)  42 us
    all_gather x1, waiting for transfers between devices, body(): queries = lax.all_gather(own_queries, 'ctx', axis=0, tiled=True)  38.8 us
    reduce_scatter x1, waiting for transfers between devices, body(): lax.psum_scatter(jnp.dot(attended, out_weight, preferred_element_type=jnp...  30.6 us
    dot_general x1, matrix products, body(): jnp.einsum('rgt,td->rgd', weights.astype(jnp.bfloat16), vals, preferred_e...  15.4 us
    reduce_sum x2, other arithmetic, body(): weight_sum = jnp.sum(weights, axis=2) + jnp.sum(tree_weights, axis=2)  15.3 us
  transfers between devices with their start and end apart: 5, of which 5 were waited for; matrix products, arithmetic and copies ran while one was open for 1% of the time, Pallas kernels for 0%

commit v1 on v0

--- a/solution.py
+++ b/solution.py
@@ -54,7 +54,10 @@
     own_queries = settled[:, :query_width].astype(jnp.bfloat16)
     tree_keys = settled[:, query_width : query_width + head_size].astype(jnp.bfloat16)
     tree_vals = settled[:, query_width + head_size :].astype(jnp.bfloat16)
-    queries = lax.all_gather(own_queries, "ctx", axis=0, tiled=True)
+    peers = lax.axis_size("ctx")
+    blocks = jnp.stack([own_queries for _ in range(peers)])
+    blocks = lax.all_to_all(blocks, "ctx", split_axis=0, concat_axis=0)
+    queries = jnp.concatenate(blocks, axis=0)
     position = lax.axis_index("ctx")
     keys = context_keys[:, 0, :]
     vals = context_values[:, 0, :]

time: 427 us -> 403 us (0.944)
  waiting for transfers between devices: 263 us -> 237 us
  starting transfers between devices: 0.17 us -> 5.02 us
    all_gather x1 -> x0, waiting for transfers between devices: 38.8 us -> none  [body(): queries = lax.all_gather(own_queries, 'ctx', axis=0, tiled=True)]
    all_to_all x0 -> x1, waiting for transfers between devices: none -> 12.5 us  [body(): blocks = lax.all_to_all(blocks, 'ctx', split_axis=0, concat_axis=0)]
    all_to_all x0 -> x1, starting transfers between devices: none -> 4.89 us  [body(): blocks = lax.all_to_all(blocks, 'ctx', split_axis=0, concat_axis=0)]
    unnamed x6 -> x5, waiting for transfers between devices: 72.2 us -> 72.3 us
where the time goes in v1:
time: 403 us; the launch traced here: 402 us
  waiting for transfers between devices  237 us (59%)
  blocking collectives  80.9 us (20%)
  matrix products  39.1 us (10%)
  other arithmetic  20.8 us (5%)
  between operations  13.3 us (3%)
  local copies, waits for them, and re-layouts  6.53 us (2%)
  starting transfers between devices  5.02 us (1%)
    reduce_scatter x1, waiting for transfers between devices, body(): reduced = lax.psum_scatter(packed, 'ctx', scatter_dimension=0, tiled=True)  79.2 us
    unnamed x5, waiting for transfers between devices  72.3 us
    pmax x1, blocking collectives, body(): highest = lax.pmax(local_high, 'ctx')  70.4 us
    all_gather x1, waiting for transfers between devices, body(): attended = lax.all_gather(own_attended, 'ctx', axis=0, tiled=True)  41.9 us
    reduce_scatter x1, waiting for transfers between devices, body(): lax.psum_scatter(jnp.dot(attended, out_weight, preferred_element_type=jnp...  30.6 us
    dot_general x1, matrix products, body(): jnp.einsum('rgt,td->rgd', weights.astype(jnp.bfloat16), vals, preferred_e...  15.4 us
    reduce_sum x2, other arithmetic, body(): weight_sum = jnp.sum(weights, axis=2) + jnp.sum(tree_weights, axis=2)  15.3 us
    dot_general x1, matrix products, body(): jnp.einsum('rgd,td->rgt', grouped, keys, preferred_element_type=jnp.float32)  13.9 us
  transfers between devices with their start and end apart: 5, of which 5 were waited for; matrix products, arithmetic and copies ran while one was open for 1% of the time, Pallas kernels for 0%

profile of v1, /device:TPU:0, one launch (start us, length us, event | category | flops | bytes accessed | tf_op | source)
XLA Modules:
  0.0 402.2 jit_solution(12428744652340282152)
XLA Ops:
  6.5 0.0 copy-start
  6.5 0.0 reduce-scatter.6.cloned.1.call-start
  6.5 10.5 %all_gather.6 = bf16[512,512]{1,0:T(8,128)(2,1)S(1)} all-gather(bf16[256,512]{1,0:T(8,128)(2,1)} %param.10), channel_id=1, replica_groups=mesh['sec'=2,'head'=4,'ctx'=16] {'sec'}, dimensions={0}, use_global_device_ids=true | all-gather | bytes 786432 | tf_op jit(solution)/shard_map/all_gather | solution.py:36
  17.0 0.7 convert_element_type.29
  17.7 0.2 fusion.12
  17.9 0.1 broadcast_select_fusion
  18.0 2.2 fusion.5
  20.3 1.8 pad_maximum_fusion
  22.1 0.0 copy-start.2
  22.1 0.0 copy-start.3
  22.1 0.0 reduce-scatter.6.cloned.1.call-update
  22.1 79.2 %reduce-scatter.6.cloned.1.call-done = f32[32,1408]{1,0:T(8,128)} async-done(((f32[512,1408]{1,0:T(8,128)}), f32[32,1408]{1,0:T(8,128)}) %reduce-scatter.6.cloned.1.call-update) | async-done | bytes 180240 | tf_op jit(solution)/shard_map/reduce_scatter | solution.py:50
  101.3 0.8 fusion.35
  102.1 1.0 fusion.32
  103.1 1.1 stack.2
  104.2 4.9 %all-to-all-start = ((bf16[16,32,1024]{2,1,0:T(8,128)(2,1)}), bf16[16,32,1024]{2,1,0:T(8,128)(2,1)S(1)}, u32[]{:S(2)}, u32[]{:S(2)}) async-start(bf16[16,32,1024]{2,1,0:T(8,128)(2,1)} %stack.2), calls=%async_computation.1 | async-start | bytes 2097152 | tf_op jit(solution)/shard_map/all_to_all | solution.py:59
  109.1 0.0 reduce-scatter.10.cloned.1.call-start
  109.2 0.0 copy-done.2
  109.2 0.1 broadcast_in_dim.76
  109.3 0.1 lt.23
  109.4 0.1 pad.2.clone
  109.5 0.0 copy-done.3
  109.5 0.6 convolution_compare_fusion.2
  110.1 1.1 convolution_compare_fusion
  111.2 0.4 convolution_compare_fusion.3
  111.6 0.7 broadcast_compare_fusion
  112.3 12.5 %all-to-all-done = bf16[16,32,1024]{2,1,0:T(8,128)(2,1)S(1)} async-done(((bf16[16,32,1024]{2,1,0:T(8,128)(2,1)}), bf16[16,32,1024]{2,1,0:T(8,128)(2,1)S(1)}, u32[]{:S(2)}, u32[]{:S(2)}) %all-to-all-start) | async-done | bytes 1048608 | tf_op jit(solution)/shard_map/all_to_all | solution.py:59
  124.8 0.0 copy-start.1
  124.8 0.3 copy.27
  125.1 0.5 select_reduce_fusion.1
  125.6 0.3 copy-done.1
  125.8 13.9 %select_reduce_fusion = (f32[512,8]{0,1:T(8,128)S(1)}, f32[512,8,2048]{2,0,1:T(8,128)}) fusion(pred[512,2048]{1,0:T(8,128)(4,1)S(1)} %broadcast_compare_fusion, bf16[2048,1,128]{2,0,1:T(8,128)(2,1)S(1)} %copy-done.1, bf16[512,8,128]{2,1,0:T(8,128)(2,1)S(1)} %bitcast.37), kind=kOutput, calls=%fused_computation.1 | convolution fusion | flops 2172645376 | bytes 36192256 | tf_op jit(solution)/shard_map/rgd,td->rgt/dot_general | solution.py:70
  139.8 70.4 %pmax.7 = f32[512,8]{0,1:T(8,128)S(1)} all-reduce(f32[512,8]{0,1:T(8,128)S(1)} %max.5), channel_id=1, replica_groups=mesh['sec'=2,'head'=4,'ctx'=16] {'ctx'}, use_global_device_ids=true, to_apply=%region_4.5 | all-reduce | flops 4096 | bytes 32768 | tf_op jit(solution)/shard_map/pmax | solution.py:79
  210.1 15.2 %fusion = f32[512,8]{0,1:T(8,128)S(1)} fusion(f32[512,8,2048]{2,0,1:T(8,128)} %get-tuple-element.6, f32[512,8]{0,1:T(8,128)S(1)} %pmax.7, pred[512,2048]{1,0:T(8,128)(4,1)S(1)} %broadcast_compare_fusion), kind=kLoop, calls=%fused_computation.2 | loop fusion | flops 33550336 | bytes 34635776 | tf_op jit(solution)/shard_map/reduce_sum | solution.py:82
  225.3 15.4 %fusion.2 = f32[512,8,128]{0,2,1:T(8,128)} fusion(f32[512,8,2048]{2,0,1:T(8,128)} %get-tuple-element.6, f32[512,8]{0,1:T(8,128)S(1)} %pmax.7, pred[512,2048]{1,0:T(8,128)(4,1)S(1)} %broadcast_compare_fusion, bf16[2048,1,128]{2,0,1:T(8,128)(2,1)} %param.17), kind=kOutput, calls=%fused_computation.4 | convolution fusion | flops 2181038080 | bytes 37240832 | tf_op jit(solution)/shard_map/rgt,td->rgd/dot_general | solution.py:83
  240.7 0.1 fusion.25
  240.9 2.1 convolution_add_fusion
  243.0 0.2 maximum_maximum_fusion
  243.2 2.0 copy.23
  245.2 0.0 reduce-scatter.10.cloned.1.call-update
  245.2 0.0 all-gather.2.cloned.1.call-start
  245.3 72.2 %reduce-scatter.10.cloned.1.call-done = f32[32,1152]{1,0:T(8,128)} async-done(((f32[512,1152]{1,0:T(8,128)}), f32[32,1152]{1,0:T(8,128)}) %reduce-scatter.10.cloned.1.call-update) | async-done | bytes 147472
  317.5 0.9 slice.36
  318.4 0.2 copy.25
  318.6 0.7 slice.37
  319.3 0.1 copy.26
  319.4 0.1 fusion.20
  319.5 0.8 copy.19
  320.2 0.0 all-gather.2.cloned.1.call-update
  320.3 0.0 reduce-scatter.8.cloned.1.call-start
  320.3 41.9 %all-gather.2.cloned.1.call-done = bf16[512,1024]{1,0:T(8,128)(2,1)} async-done(((bf16[32,1024]{1,0:T(8,128)(2,1)}), bf16[512,1024]{1,0:T(8,128)(2,1)}) %all-gather.2.cloned.1.call-update) | async-done | bytes 1048592 | tf_op jit(solution)/shard_map/all_gather | solution.py:104
  362.2 0.0 copy-done
  362.2 2.8 convolution_convert_fusion
  365.0 0.0 reduce-scatter.8.cloned.1.call-update
  365.0 30.6 %reduce-scatter.8.cloned.1.call-done = bf16[64,512]{1,0:T(8,128)(2,1)} async-done(((bf16[512,512]{1,0:T(8,128)(2,1)}), bf16[64,512]{1,0:T(8,128)(2,1)}) %reduce-scatter.8.cloned.1.call-update) | async-done | bytes 65552 | tf_op jit(solution)/shard_map/reduce_scatter | solution.py:105
  (6 shorter events, 0.0 us)
Async XLA Ops:
  6.5 355.7 %copy-start = (bf16[1024,512]{1,0:T(8,128)(2,1)S(1)}, bf16[1024,512]{1,0:T(8,128)(2,1)}, u32[]{:S(2)}) copy-start(bf16[1024,512]{1,0:T(8,128)(2,1)} %param.15) | copy-start | bytes 3145732
  6.5 94.7 %reduce-scatter.6.cloned.1.call-start = ((), (), s32[]{:S(2)}) async-start(), calls=%async_computation.4 | async-start | bytes 3063808 | tf_op jit(solution)/shard_map/reduce_scatter | solution.py:50
  22.1 87.2 %copy-start.2 = (s32[32]{0:T(128)S(1)}, s32[32]{0:T(128)}, u32[]{:S(2)}) copy-start(s32[32]{0:T(128)} %param.18) | copy-start | bytes 388
  22.1 87.4 %copy-start.3 = (s32[512]{0:T(512)S(1)}, s32[512]{0:T(512)}, u32[]{:S(2)}) copy-start(s32[512]{0:T(512)} %param.19) | copy-start | bytes 6148
  104.2 20.6 %all-to-all-start = ((bf16[16,32,1024]{2,1,0:T(8,128)(2,1)}), bf16[16,32,1024]{2,1,0:T(8,128)(2,1)S(1)}, u32[]{:S(2)}, u32[]{:S(2)}) async-start(bf16[16,32,1024]{2,1,0:T(8,128)(2,1)} %stack.2), calls=%async_computation.1 | async-start | bytes 2097152 | tf_op jit(solution)/shard_map/all_to_all | solution.py:59
  109.1 208.4 %reduce-scatter.10.cloned.1.call-start = ((), (), s32[]{:S(2)}) async-start(), calls=%async_computation.7 | async-start | bytes 2506752
  124.8 1.0 copy-start.1
  245.2 117.0 %all-gather.2.cloned.1.call-start = ((), (), s32[]{:S(2)}) async-start(), calls=%async_computation.5 | async-start | bytes 1114112 | tf_op jit(solution)/shard_map/all_gather | solution.py:104
  320.3 75.4 %reduce-scatter.8.cloned.1.call-start = ((), (), s32[]{:S(2)}) async-start(), calls=%async_computation.6 | async-start | bytes 589824 | tf_op jit(solution)/shard_map/reduce_scatter | solution.py:105
Sparse Core Ops, SparseCore 0:
  22.2 79.0 reduce-scatter.5
  245.3 72.1 reduce-scatter.9
  320.4 41.8 all-gather.1
  365.1 30.4 reduce-scatter.7
